TPU v7x, 32 devices: a whole 2x2x4 slice. The times are simulated.
32 devices in a mesh: sum: 8 (over z, x), mode: 4 (over y, core).
Axes of the slice: x: 2, y: 2, z: 4, core: 2. Of those that a mesh axis runs over, the one named last changes fastest.
Arguments:
- left_cores: bfloat16 [8, 512, 64, 512], P('sum', None, 'mode'), may hold values from -80 to 80, as said below
- right_cores: bfloat16 [8, 512, 64, 512], P('sum', None, 'mode'), may hold values from -6 to 6
- sketch: bfloat16 [64, 512, 512], P('mode'), may hold values from -0.03125 to 0.03125
Outputs:
- basis_core: float32 [512, 64, 512], P('sum', 'mode')
- carries: float32 [8, 512, 512], P('sum')
Inputs may be any that keep to these rules, and one draw needn't show every extreme that they name: `left_cores`: independent entries; each row (summand, left rank, mode index) has its own scale.
All inputs are finite; a program needn't handle non-finite values.
Results may differ from a plain program's by a relative error of at most 0.0035.
Values may be sent and summed in bfloat16 or wider, within the bound.
No kernel may reach another device: no remote copies, remote signals or barrier semaphores. Data moves between devices by JAX's collectives and lax.ppermute only.
A program may use at most 128 MiB of HBM per device.

v0:
```python
import math
import jax
import jax.numpy as jnp
from jax import lax
from jax.experimental.layout import Layout, with_layout_constraint
from jax.sharding import PartitionSpec as P

R_IN = 512
MODES = 64
BLOCK = 128
HI = lax.Precision.HIGHEST


def mm(a, b):
    return jnp.dot(a, b, precision=HI, preferred_element_type=jnp.float32)


def orthonormal(sketched, gram):
    n = gram.shape[0]
    b = min(BLOCK, n)
    nb = n // b
    eye = jnp.eye(b, dtype=jnp.float32)
    inverses = []
    panels = []
    trailing = gram
    for k in range(nb):
        diag = trailing[:b, :b]
        lkk = jnp.linalg.cholesky(diag)
        ikk = lax.linalg.triangular_solve(lkk, eye, left_side=True, lower=True)
        inverses.append(ikk)
        if k < nb - 1:
            panel = mm(trailing[b:, :b], ikk.T)
            panels.append(panel)
            trailing = trailing[b:, b:] - mm(panel, panel.T)
    blocks = []
    for k in range(nb):
        rhs = sketched[:, k * b : (k + 1) * b]
        if k > 0:
            done = jnp.concatenate(blocks, axis=1)
            lrow = jnp.concatenate(
                [panels[j][(k - j - 1) * b : (k - j) * b] for j in range(k)], axis=1
            )
            rhs = rhs - mm(done, lrow.T)
        blocks.append(mm(rhs, inverses[k].T))
    return jnp.concatenate(blocks, axis=1)


def per_device(left_cores, right_cores, sketch):
    sum_local, rows_in, mode_local, rank_width = left_cores.shape
    target = sketch.shape[2]
    partial_map = lax.dot_general(
        right_cores, sketch, (((2, 3), (0, 1)), ((), ())), preferred_element_type=jnp.float32
    )
    mapped = lax.psum(partial_map, "mode").astype(jnp.bfloat16)
    local_sum = lax.dot_general(
        left_cores, mapped, (((0, 3), (0, 1)), ((), ())), preferred_element_type=jnp.float32
    )
    local_sum = with_layout_constraint(local_sum, Layout(major_to_minor=(0, 1, 2)))
    factor = math.sqrt(R_IN * MODES)
    share = lax.psum_scatter(local_sum, "sum", scatter_dimension=0, tiled=True)
    flat_share = share.reshape(-1, target)
    gram_part = jnp.dot(flat_share.T, flat_share, precision=HI)
    gram = lax.psum(gram_part, ("sum", "mode"))
    basis = orthonormal(flat_share, gram)
    block = basis.reshape(share.shape)
    rounded = block.astype(jnp.bfloat16)
    pieces = lax.all_gather(rounded, "sum", axis=0, tiled=True)
    partial_carry = lax.dot_general(
        pieces, left_cores, (((0, 1), (1, 2)), ((), ())), preferred_element_type=jnp.float32
    )
    partial_carry = jnp.transpose(partial_carry, (1, 0, 2))
    carries = lax.psum(partial_carry, "mode")
    return (block * factor, carries)


def solution(mesh):
    in_specs = (P("sum", None, "mode", None), P("sum", None, "mode", None), P("mode", None, None))
    out_specs = (P("sum", "mode", None), P("sum", None, None))
    return jax.shard_map(
        per_device, mesh=mesh, in_specs=in_specs, out_specs=out_specs, check_vma=False
    )
```

profile of v0, /device:TPU:0, one launch (start us, length us, event | category | flops | bytes accessed | tf_op | source)
XLA Modules:
  0.0 789.0 jit_solution(3310593755060591880)
XLA Ops:
  7.2 17.1 %fusion.10 = f32[1,512,512]{2,1,0:T(8,128)S(1)} fusion(bf16[16,512,512]{2,1,0:T(8,128)(2,1)} %param.8, bf16[512,16,512]{2,1,0:T(8,128)(2,1)} %bitcast.84), kind=kOutput, calls=%fused_computation.13 | convolution fusion | flops 4294967296 | bytes 17825792 | tf_op jit(solution)/shard_map/dot_general | solution.py:51
  24.3 28.0 %all-reduce.7 = bf16[1,512,512]{2,1,0:T(8,128)(2,1)S(1)} all-reduce(f32[1,512,512]{2,1,0:T(8,128)S(1)} %fusion.10), channel_id=1, replica_groups=mesh['sum'=8,'mode'=4] {'mode'}, use_global_device_ids=true, to_apply=%region_0.0 | all-reduce | flops 262144 | bytes 1572864 | tf_op jit(solution)/shard_map/psum | solution.py:54
  52.3 11.6 %convolution_bitcast_fusion = f32[512,16,512]{2,1,0:T(8,128)} fusion(bf16[1,512,512]{2,1,0:T(8,128)(2,1)S(1)} %all-reduce.7, bf16[1,512,16,512]{3,2,1,0:T(8,128)(2,1)} %param.6), kind=kOutput, calls=%fused_computation | convolution fusion | flops 4294967296 | bytes 25690112 | tf_op jit(solution)/shard_map/dot_general | solution.py:55
  64.3 282.3 %reduce-scatter.2.cloned.1.call-done = f32[64,16,512]{2,1,0:T(8,128)} async-done(((f32[512,16,512]{2,1,0:T(8,128)}), f32[64,16,512]{2,1,0:T(8,128)}) %reduce-scatter.2.cloned.1.call-update) | async-done | bytes 2097168 | tf_op jit(solution)/shard_map/reduce_scatter | solution.py:60
  346.6 6.7 convolution_bitcast_fusion.1
  353.4 129.0 %all-reduce.4.cloned.1.call-done = f32[512,512]{0,1:T(8,128)} async-done(((f32[512,512]{0,1:T(8,128)}), f32[512,512]{0,1:T(8,128)}) %all-reduce.4.cloned.1.call-update) | async-done | bytes 1048592 | tf_op jit(solution)/shard_map/psum | solution.py:63
  482.4 0.8 slice.79
  483.3 0.9 fusion.62
  484.2 11.7 %cholesky.74 = f32[128,128]{1,0:T(8,128)S(1)} custom-call(f32[128,128]{1,0:T(8,128)S(1)} %fusion.62), custom_call_target="Cholesky" | custom-call | tf_op jit(solution)/shard_map/jit(cholesky)/cholesky | solution.py:28
  497.2 9.8 %custom-call.8 = f32[1,128,128]{1,2,0:T(8,128)S(1)} custom-call(f32[1,128,128]{2,1,0:T(8,128)S(1)} %fusion.48), custom_call_target="InvertDiagBlocksLowerTriangular" | custom-call | tf_op jit(solution)/shard_map/triangular_solve/custom-call.0 | solution.py:29
  507.4 1.2 fusion.28
  508.6 1.7 convolution_subtract_fusion
  510.5 11.7 %cholesky.85 = f32[128,128]{1,0:T(8,128)S(1)} custom-call(f32[128,128]{1,0:T(8,128)S(1)} %fusion.60), custom_call_target="Cholesky" | custom-call | tf_op jit(solution)/shard_map/jit(cholesky)/cholesky | solution.py:28
  523.5 18.5 %custom-call.9 = f32[1,128,128]{1,2,0:T(8,128)S(1)} custom-call(f32[1,128,128]{2,1,0:T(8,128)S(1)} %fusion.49), custom_call_target="InvertDiagBlocksLowerTriangular" | custom-call | tf_op jit(solution)/shard_map/triangular_solve/custom-call.0 | solution.py:29
  543.1 0.7 fusion.66
  543.9 11.7 %cholesky.96 = f32[128,128]{1,0:T(8,128)S(1)} custom-call(f32[128,128]{1,0:T(8,128)S(1)} %fusion.58), custom_call_target="Cholesky" | custom-call | tf_op jit(solution)/shard_map/jit(cholesky)/cholesky | solution.py:28
  555.6 0.7 compare_reduce_fusion.1
  556.9 9.8 %custom-call.10 = f32[1,128,128]{1,2,0:T(8,128)S(1)} custom-call(f32[1,128,128]{2,1,0:T(8,128)S(1)} %fusion.50), custom_call_target="InvertDiagBlocksLowerTriangular" | custom-call | tf_op jit(solution)/shard_map/triangular_solve/custom-call.0 | solution.py:29
  567.6 11.9 %cholesky.107 = f32[128,128]{1,0:T(8,128)S(1)} custom-call(f32[128,128]{1,0:T(8,128)S(1)} %fusion.56), custom_call_target="Cholesky" | custom-call | tf_op jit(solution)/shard_map/jit(cholesky)/cholesky | solution.py:28
  579.6 0.7 compare_reduce_fusion
  580.9 9.8 %custom-call.11 = f32[1,128,128]{1,2,0:T(8,128)S(1)} custom-call(f32[1,128,128]{2,1,0:T(8,128)S(1)} %fusion.51), custom_call_target="InvertDiagBlocksLowerTriangular" | custom-call | tf_op jit(solution)/shard_map/triangular_solve/custom-call.0 | solution.py:29
  591.6 1.0 convolution_subtract_fusion.2
  593.3 2.7 convolution_subtract_fusion.1
  596.6 2.8 fusion.16
  600.0 0.8 copy-done.2
  601.5 1.5 copy.36
  603.4 123.7 %all-gather.2.cloned.1.call-done = bf16[512,16,512]{2,0,1:T(8,128)(2,1)} async-done(((bf16[64,16,512]{2,0,1:T(8,128)(2,1)}), bf16[512,16,512]{2,0,1:T(8,128)(2,1)}) %all-gather.2.cloned.1.call-update) | async-done | bytes 8388624 | tf_op jit(solution)/shard_map/all_gather | solution.py:67
  727.1 18.2 %fusion.13 = f32[1,512,512]{2,1,0:T(8,128)} fusion(bf16[512,16,512]{2,0,1:T(8,128)(2,1)} %all-gather.2.cloned.1.call-done, bf16[512,16,512]{2,1,0:T(8,128)(2,1)} %bitcast.85), kind=kOutput, calls=%fused_computation.14 | convolution fusion | flops 4294967296 | bytes 17825792 | tf_op jit(solution)/shard_map/dot_general | solution.py:68
  745.3 1.5 fusion.20
  746.8 1.8 copy.34
  748.6 31.2 %all-reduce.6.cloned.1.call-done = f32[1,512,512]{2,1,0:T(8,128)} async-done(((f32[1,512,512]{2,1,0:T(8,128)}), f32[1,512,512]{2,1,0:T(8,128)}) %all-reduce.6.cloned.1.call-update) | async-done | bytes 1048592 | tf_op jit(solution)/shard_map/psum | solution.py:72
  779.8 2.3 copy.59
  (48 shorter events, 10.7 us)
Async XLA Ops:
  7.2 339.5 %reduce-scatter.2.cloned.1.call-start = ((), (), s32[]{:S(2)}) async-start(), calls=%async_computation.1 | async-start | bytes 18874368 | tf_op jit(solution)/shard_map/reduce_scatter | solution.py:60
  64.0 418.4 %all-reduce.4.cloned.1.call-start = ((), (), s32[]{:S(2)}) async-start(), calls=%async_computation.2 | async-start | bytes 2097152 | tf_op jit(solution)/shard_map/psum | solution.py:63
  353.4 373.8 %all-gather.2.cloned.1.call-start = ((), (), s32[]{:S(2)}) async-start(), calls=%async_computation.3 | async-start | bytes 9437184 | tf_op jit(solution)/shard_map/all_gather | solution.py:67
  510.4 80.6 %copy-start = (f32[64,16,512]{2,1,0:T(8,128)S(1)}, f32[64,16,512]{2,1,0:T(8,128)}, u32[]{:S(2)}) copy-start(f32[64,16,512]{2,1,0:T(8,128)} %reduce-scatter.2.cloned.1.call-done) | copy-start | bytes 6291460
  592.6 3.9 copy-start.3
  596.6 3.4 copy-start.1
  600.0 0.8 copy-start.2
  603.1 176.7 %all-reduce.6.cloned.1.call-start = ((), (), s32[]{:S(2)}) async-start(), calls=%async_computation.4 | async-start | bytes 2097152 | tf_op jit(solution)/shard_map/psum | solution.py:72
Sparse Core Ops, SparseCore 0:
  64.1 282.4 reduce-scatter.1
  353.5 128.8 all-reduce.3
  603.2 123.8 all-gather.1
  745.4 34.2 all-reduce.5
where the time goes:
time: 796 us; the launch traced here: 789 us
  waiting for transfers between devices  566 us (71%)
  other arithmetic  103 us (13%)
  matrix products  67.8 us (9%)
  blocking collectives  28 us (4%)
  between operations  14.6 us (2%)
  local copies, waits for them, and re-layouts  8.84 us (1%)
    reduce_scatter x1, waiting for transfers between devices, per_device(): share = lax.psum_scatter(local_sum, 'sum', scatter_dimension=0, tiled=True)  282 us
    psum x1, waiting for transfers between devices, per_device(): gram = lax.psum(gram_part, ('sum', 'mode'))  129 us
    all_gather x1, waiting for transfers between devices, per_device(): pieces = lax.all_gather(rounded, 'sum', axis=0, tiled=True)  124 us
    another operation x8, other arithmetic, orthonormal(): ikk = lax.linalg.triangular_solve(lkk, eye, left_side=True, lower=True)  50.5 us
    another operation x12, other arithmetic, orthonormal(): lkk = jnp.linalg.cholesky(diag)  49.8 us
    psum x1, waiting for transfers between devices, per_device(): carries = lax.psum(partial_carry, 'mode')  31.2 us
    psum x1, blocking collectives, per_device(): mapped = lax.psum(partial_map, 'mode').astype(jnp.bfloat16)  28 us
    dot_general x1, matrix products, per_device(): lax.dot_general(pieces, left_cores, (((0, 1), (1, 2)), ((), ())), preferr...  18.2 us
  transfers between devices with their start and end apart: 4, of which 4 were waited for; matrix products, arithmetic and copies ran while one was open for 0% of the time, Pallas kernels for 0%

commit v1 on v0

--- a/solution.py
+++ b/solution.py
@@ -64,7 +64,14 @@
     basis = orthonormal(flat_share, gram)
     block = basis.reshape(share.shape)
     rounded = block.astype(jnp.bfloat16)
-    pieces = lax.all_gather(rounded, "sum", axis=0, tiled=True)
+    n_dev = lax.axis_size("sum")
+    right = [(i, (i + 1) % n_dev) for i in range(n_dev)]
+    parts = [rounded]
+    for stride in range(1, n_dev):
+        parts = [lax.ppermute(parts[0], "sum", right), *parts]
+    whole = jnp.concatenate(parts, axis=0)
+    shift = (lax.axis_index("sum") + 1) * parts[-1].shape[0]
+    pieces = jnp.roll(whole, shift, axis=0)
     partial_carry = lax.dot_general(
         pieces, left_cores, (((0, 1), (1, 2)), ((), ())), preferred_element_type=jnp.float32
     )

time: 796 us -> 882 us (1.11)
  local copies, waits for them, and re-layouts: 8.84 us -> 73.1 us
  waiting for transfers between devices: 566 us -> 580 us
  starting transfers between devices: 0.67 us -> 13 us
    ppermute x0 -> x7, waiting for transfers between devices: none -> 146 us  [per_device(): parts = [lax.ppermute(parts[0], 'sum', right), *parts]]
    all_gather x1 -> x0, waiting for transfers between devices: 124 us -> none  [per_device(): pieces = lax.all_gather(rounded, 'sum', axis=0, tiled=True)]
    concatenate x0 -> x1, local copies, waits for them, and re-layouts: none -> 37.5 us  [per_device(): pieces = jnp.roll(whole, shift, axis=0)]
    ppermute x0 -> x7, local copies, waits for them, and re-layouts: none -> 22 us  [per_device(): parts = [lax.ppermute(parts[0], 'sum', right), *parts]]
    reduce_scatter x1, waiting for transfers between devices: 282 us -> 271 us  [per_device(): share = lax.psum_scatter(local_sum, 'sum', scatter_dimension=0, tiled=True)]
    psum x1, starting transfers between devices: 0.3 us -> 11.2 us  [per_device(): gram = lax.psum(gram_part, ('sum', 'mode'))]
  transfers between devices with their start and end apart: 4 -> 10, of which waited for: 4 -> 10; matrix products, arithmetic and copies ran while one was open for 0% -> 3% of each run, Pallas kernels for 0% -> 0%
where the time goes in v1:
time: 882 us; the launch traced here: 871 us
  waiting for transfers between devices  580 us (66%)
  other arithmetic  94.7 us (11%)
  local copies, waits for them, and re-layouts  73.1 us (8%)
  matrix products  67.3 us (8%)
  blocking collectives  28 us (3%)
  between operations  14.6 us (2%)
  starting transfers between devices  13 us (1%)
    reduce_scatter x1, waiting for transfers between devices, per_device(): share = lax.psum_scatter(local_sum, 'sum', scatter_dimension=0, tiled=True)  271 us
    ppermute x7, waiting for transfers between devices, per_device(): parts = [lax.ppermute(parts[0], 'sum', right), *parts]  146 us
    psum x1, waiting for transfers between devices, per_device(): gram = lax.psum(gram_part, ('sum', 'mode'))  129 us
    another operation x12, other arithmetic, orthonormal(): lkk = jnp.linalg.cholesky(diag)  49.9 us
    another operation x8, other arithmetic, orthonormal(): ikk = lax.linalg.triangular_solve(lkk, eye, left_side=True, lower=True)  42.3 us
    concatenate x1, local copies, waits for them, and re-layouts, per_device(): pieces = jnp.roll(whole, shift, axis=0)  37.5 us
    psum x1, waiting for transfers between devices, per_device(): carries = lax.psum(partial_carry, 'mode')  33.2 us
    psum x1, blocking collectives, per_device(): mapped = lax.psum(partial_map, 'mode').astype(jnp.bfloat16)  28 us
  transfers between devices with their start and end apart: 10, of which 10 were waited for; matrix products, arithmetic and copies ran while one was open for 3% of the time, Pallas kernels for 0%

profile of v1, /device:TPU:0, one launch (start us, length us, event | category | flops | bytes accessed | tf_op | source)
XLA Modules:
  0.0 870.6 jit_solution(498127510226466390)
XLA Ops:
  7.2 17.1 %fusion.16 = f32[1,512,512]{2,1,0:T(8,128)S(1)} fusion(bf16[16,512,512]{2,1,0:T(8,128)(2,1)} %param.8, bf16[512,16,512]{2,1,0:T(8,128)(2,1)} %bitcast.84), kind=kOutput, calls=%fused_computation.15 | convolution fusion | flops 4294967296 | bytes 17825792 | tf_op jit(solution)/shard_map/dot_general | solution.py:51
  24.3 28.0 %all-reduce.7 = bf16[1,512,512]{2,1,0:T(8,128)(2,1)S(1)} all-reduce(f32[1,512,512]{2,1,0:T(8,128)S(1)} %fusion.16), channel_id=1, replica_groups=mesh['sum'=8,'mode'=4] {'mode'}, use_global_device_ids=true, to_apply=%region_0.0 | all-reduce | flops 262144 | bytes 1572864 | tf_op jit(solution)/shard_map/psum | solution.py:54
  52.3 11.6 %convolution_bitcast_fusion = f32[512,16,512]{2,1,0:T(8,128)} fusion(bf16[1,512,512]{2,1,0:T(8,128)(2,1)S(1)} %all-reduce.7, bf16[1,512,16,512]{3,2,1,0:T(8,128)(2,1)} %param.6), kind=kOutput, calls=%fused_computation | convolution fusion | flops 4294967296 | bytes 25690112 | tf_op jit(solution)/shard_map/dot_general | solution.py:55
  64.0 11.2 %all-reduce.4.cloned.1.call-start = ((), (), s32[]{:S(2)}) async-start(), calls=%async_computation.2 | async-start | bytes 2097152 | tf_op jit(solution)/shard_map/psum | solution.py:63
  75.2 271.3 %reduce-scatter.2.cloned.1.call-done = f32[64,16,512]{2,1,0:T(8,128)} async-done(((f32[512,16,512]{2,1,0:T(8,128)}), f32[64,16,512]{2,1,0:T(8,128)}) %reduce-scatter.2.cloned.1.call-update) | async-done | bytes 2097168 | tf_op jit(solution)/shard_map/reduce_scatter | solution.py:60
  346.5 6.7 convolution_bitcast_fusion.1
  353.3 129.0 %all-reduce.4.cloned.1.call-done = f32[512,512]{0,1:T(8,128)} async-done(((f32[512,512]{0,1:T(8,128)}), f32[512,512]{0,1:T(8,128)}) %all-reduce.4.cloned.1.call-update) | async-done | bytes 1048592 | tf_op jit(solution)/shard_map/psum | solution.py:63
  484.2 11.7 %cholesky.74 = f32[128,128]{1,0:T(8,128)S(1)} custom-call(f32[128,128]{1,0:T(8,128)S(1)} %fusion.65), custom_call_target="Cholesky" | custom-call | tf_op jit(solution)/shard_map/jit(cholesky)/cholesky | solution.py:28
  497.2 9.8 %custom-call.8 = f32[1,128,128]{1,2,0:T(8,128)S(1)} custom-call(f32[1,128,128]{2,1,0:T(8,128)S(1)} %fusion.51), custom_call_target="InvertDiagBlocksLowerTriangular" | custom-call | tf_op jit(solution)/shard_map/triangular_solve/custom-call.0 | solution.py:29
  510.5 11.7 %cholesky.85 = f32[128,128]{1,0:T(8,128)S(1)} custom-call(f32[128,128]{1,0:T(8,128)S(1)} %fusion.63), custom_call_target="Cholesky" | custom-call | tf_op jit(solution)/shard_map/jit(cholesky)/cholesky | solution.py:28
  523.5 10.2 %custom-call.9 = f32[1,128,128]{1,2,0:T(8,128)S(1)} custom-call(f32[1,128,128]{2,1,0:T(8,128)S(1)} %fusion.52), custom_call_target="InvertDiagBlocksLowerTriangular" | custom-call | tf_op jit(solution)/shard_map/triangular_solve/custom-call.0 | solution.py:29
  535.5 11.7 %cholesky.96 = f32[128,128]{1,0:T(8,128)S(1)} custom-call(f32[128,128]{1,0:T(8,128)S(1)} %fusion.61), custom_call_target="Cholesky" | custom-call | tf_op jit(solution)/shard_map/jit(cholesky)/cholesky | solution.py:28
  548.7 9.8 %custom-call.10 = f32[1,128,128]{1,2,0:T(8,128)S(1)} custom-call(f32[1,128,128]{2,1,0:T(8,128)S(1)} %fusion.53), custom_call_target="InvertDiagBlocksLowerTriangular" | custom-call | tf_op jit(solution)/shard_map/triangular_solve/custom-call.0 | solution.py:29
  559.4 11.9 %cholesky.107 = f32[128,128]{1,0:T(8,128)S(1)} custom-call(f32[128,128]{1,0:T(8,128)S(1)} %fusion.59), custom_call_target="Cholesky" | custom-call | tf_op jit(solution)/shard_map/jit(cholesky)/cholesky | solution.py:28
  572.7 9.8 %custom-call.11 = f32[1,128,128]{1,2,0:T(8,128)S(1)} custom-call(f32[1,128,128]{2,1,0:T(8,128)S(1)} %fusion.54), custom_call_target="InvertDiagBlocksLowerTriangular" | custom-call | tf_op jit(solution)/shard_map/triangular_solve/custom-call.0 | solution.py:29
  588.4 2.8 fusion.19
  594.9 25.3 %collective-permute-done = bf16[64,16,512]{2,1,0:T(8,128)(2,1)S(1)} collective-permute-done((bf16[64,16,512]{2,1,0:T(8,128)(2,1)S(1)}, bf16[64,16,512]{2,1,0:T(8,128)(2,1)S(1)}, u32[]{:S(2)}, u32[]{:S(2)}) %collective-permute-start) | collective-permute-done | bytes 1048608 | tf_op jit(solution)/shard_map/ppermute | solution.py:71
  620.2 25.8 %collective-permute-done.1 = bf16[64,16,512]{2,1,0:T(8,128)(2,1)S(1)} collective-permute-done((bf16[64,16,512]{2,1,0:T(8,128)(2,1)S(1)}, bf16[64,16,512]{2,1,0:T(8,128)(2,1)S(1)}, u32[]{:S(2)}, u32[]{:S(2)}) %collective-permute-start.1) | collective-permute-done | bytes 1048608 | tf_op jit(solution)/shard_map/ppermute | solution.py:71
  647.0 24.9 %collective-permute-done.2 = bf16[64,16,512]{2,1,0:T(8,128)(2,1)S(1)} collective-permute-done((bf16[64,16,512]{2,1,0:T(8,128)(2,1)S(1)}, bf16[64,16,512]{2,1,0:T(8,128)(2,1)S(1)}, u32[]{:S(2)}, u32[]{:S(2)}) %collective-permute-start.2) | collective-permute-done | bytes 1048608 | tf_op jit(solution)/shard_map/ppermute | solution.py:71
  672.9 24.0 %collective-permute-done.3 = bf16[64,16,512]{2,1,0:T(8,128)(2,1)S(1)} collective-permute-done((bf16[64,16,512]{2,1,0:T(8,128)(2,1)S(1)}, bf16[64,16,512]{2,1,0:T(8,128)(2,1)S(1)}, u32[]{:S(2)}, u32[]{:S(2)}) %collective-permute-start.3) | collective-permute-done | bytes 1048608 | tf_op jit(solution)/shard_map/ppermute | solution.py:71
  697.8 23.0 %collective-permute-done.4 = bf16[64,16,512]{2,1,0:T(8,128)(2,1)S(1)} collective-permute-done((bf16[64,16,512]{2,1,0:T(8,128)(2,1)S(1)}, bf16[64,16,512]{2,1,0:T(8,128)(2,1)S(1)}, u32[]{:S(2)}, u32[]{:S(2)}) %collective-permute-start.4) | collective-permute-done | bytes 1048608 | tf_op jit(solution)/shard_map/ppermute | solution.py:71
  721.8 22.9 %collective-permute-done.5 = bf16[64,16,512]{2,1,0:T(8,128)(2,1)} collective-permute-done((bf16[64,16,512]{2,1,0:T(8,128)(2,1)S(1)}, bf16[64,16,512]{2,1,0:T(8,128)(2,1)}, u32[]{:S(2)}, u32[]{:S(2)}) %collective-permute-start.5) | collective-permute-done | bytes 1048608 | tf_op jit(solution)/shard_map/ppermute | solution.py:71
  747.4 3.2 copy.59
  750.6 3.1 copy.58
  753.7 3.2 copy.57
  756.9 3.1 copy.56
  760.0 3.1 copy.55
  763.1 3.1 copy.54
  766.5 3.1 copy.53
  769.7 37.5 %concatenate.26 = bf16[1024,16,512]{0,2,1:T(8,128)(2,1)} concatenate(bf16[64,16,512]{0,2,1:T(8,128)(2,1)} %copy.53, bf16[64,16,512]{0,2,1:T(8,128)(2,1)} %copy.54, bf16[64,16,512]{0,2,1:T(8,128)(2,1)} %copy.55, bf16[64,16,512]{0,2,1:T(8,128)(2,1)} %copy.56, bf16[64,16,512]{0,2,1:T(8,128)(2,1)} %copy.57, bf16[64,16,512]{0,2,1:T(8,128)(2,1)} %copy.58, bf16[64,16,512]{0,2,1:T(8,128)(2,1)} %copy.59, ...), dimensions={0} | concatenate | bytes 33554432 | tf_op jit(solution)/shard_map/jit(_roll_dynamic)/concatenate | solution.py:74
  807.2 17.7 %fusion.11 = f32[1,512,512]{2,1,0:T(8,128)} fusion(bf16[512,16,512]{2,1,0:T(8,128)(2,1)} %bitcast.85, bf16[1024,16,512]{0,2,1:T(8,128)(2,1)} %concatenate.26, s32[]{:T(128)S(6)} %select_n.17), kind=kOutput, calls=%fused_computation.13 | convolution fusion | flops 4294967296 | bytes 17825796 | tf_op jit(solution)/shard_map/dot_general | solution.py:75
  828.1 33.2 %all-reduce.6.cloned.1.call-done = f32[1,512,512]{2,1,0:T(8,128)} async-done(((f32[1,512,512]{2,1,0:T(8,128)}), f32[1,512,512]{2,1,0:T(8,128)}) %all-reduce.6.cloned.1.call-update) | async-done | bytes 1048592 | tf_op jit(solution)/shard_map/psum | solution.py:79
  (79 shorter events, 35.3 us)
Async XLA Ops:
  7.2 339.4 %reduce-scatter.2.cloned.1.call-start = ((), (), s32[]{:S(2)}) async-start(), calls=%async_computation.1 | async-start | bytes 18874368 | tf_op jit(solution)/shard_map/reduce_scatter | solution.py:60
  64.0 418.4 %all-reduce.4.cloned.1.call-start = ((), (), s32[]{:S(2)}) async-start(), calls=%async_computation.2 | async-start | bytes 2097152 | tf_op jit(solution)/shard_map/psum | solution.py:63
  353.3 508.1 %all-reduce.6.cloned.1.call-start = ((), (), s32[]{:S(2)}) async-start(), calls=%async_computation.3 | async-start | bytes 2097152 | tf_op jit(solution)/shard_map/psum | solution.py:79
  510.3 72.5 %copy-start = (f32[64,16,512]{2,1,0:T(8,128)S(1)}, f32[64,16,512]{2,1,0:T(8,128)}, u32[]{:S(2)}) copy-start(f32[64,16,512]{2,1,0:T(8,128)} %reduce-scatter.2.cloned.1.call-done) | copy-start | bytes 6291460
  584.4 3.9 copy-start.9
  588.4 3.4 copy-start.1
  591.8 0.9 copy-start.2
  593.4 151.6 %copy-start.3 = (bf16[1024,512]{1,0:T(8,128)(2,1)}, bf16[1024,512]{1,0:T(8,128)(2,1)S(1)}, u32[]{:S(2)}) copy-start(bf16[1024,512]{1,0:T(8,128)(2,1)S(1)} %copy.52) | copy-start | bytes 3145732
  593.4 26.8 %collective-permute-start = (bf16[64,16,512]{2,1,0:T(8,128)(2,1)S(1)}, bf16[64,16,512]{2,1,0:T(8,128)(2,1)S(1)}, u32[]{:S(2)}, u32[]{:S(2)}) collective-permute-start(bf16[64,16,512]{2,1,0:T(8,128)(2,1)S(1)} %bitcast.81), channel_id=1, source_target_pairs={{0,4},{4,8},{8,12},{12,16},{16,20},{20,24},{24,28},{28,0},{1,5},{5... | collective-permute-start | bytes 3145736 | tf_op jit(solution)/shard_map/ppermute | solution.py:71
  620.2 124.8 %copy-start.4 = (bf16[64,16,512]{2,1,0:T(8,128)(2,1)}, bf16[64,16,512]{2,1,0:T(8,128)(2,1)S(1)}, u32[]{:S(2)}) copy-start(bf16[64,16,512]{2,1,0:T(8,128)(2,1)S(1)} %collective-permute-done) | copy-start | bytes 3145732
  620.2 25.8 %collective-permute-start.1 = (bf16[64,16,512]{2,1,0:T(8,128)(2,1)S(1)}, bf16[64,16,512]{2,1,0:T(8,128)(2,1)S(1)}, u32[]{:S(2)}, u32[]{:S(2)}) collective-permute-start(bf16[64,16,512]{2,1,0:T(8,128)(2,1)S(1)} %collective-permute-done), channel_id=1, source_target_pairs={{0,4},{4,8},{8,12},{12,16},{16,20},{20,24},{24,28},{28,0},{1,5},{5... | collective-permute-start | bytes 3145736 | tf_op jit(solution)/shard_map/ppermute | solution.py:71
  646.0 1.0 copy-start.5
  647.0 24.9 %collective-permute-start.2 = (bf16[64,16,512]{2,1,0:T(8,128)(2,1)S(1)}, bf16[64,16,512]{2,1,0:T(8,128)(2,1)S(1)}, u32[]{:S(2)}, u32[]{:S(2)}) collective-permute-start(bf16[64,16,512]{2,1,0:T(8,128)(2,1)S(1)} %collective-permute-done.1), channel_id=1, source_target_pairs={{0,4},{4,8},{8,12},{12,16},{16,20},{20,24},{24,28},{28,0},{1,5},{5... | collective-permute-start | bytes 3145736 | tf_op jit(solution)/shard_map/ppermute | solution.py:71
  671.9 1.0 copy-start.6
  672.9 24.0 %collective-permute-start.3 = (bf16[64,16,512]{2,1,0:T(8,128)(2,1)S(1)}, bf16[64,16,512]{2,1,0:T(8,128)(2,1)S(1)}, u32[]{:S(2)}, u32[]{:S(2)}) collective-permute-start(bf16[64,16,512]{2,1,0:T(8,128)(2,1)S(1)} %collective-permute-done.2), channel_id=1, source_target_pairs={{0,4},{4,8},{8,12},{12,16},{16,20},{20,24},{24,28},{28,0},{1,5},{5... | collective-permute-start | bytes 3145736 | tf_op jit(solution)/shard_map/ppermute | solution.py:71
  696.9 1.0 copy-start.7
  697.8 23.0 %collective-permute-start.4 = (bf16[64,16,512]{2,1,0:T(8,128)(2,1)S(1)}, bf16[64,16,512]{2,1,0:T(8,128)(2,1)S(1)}, u32[]{:S(2)}, u32[]{:S(2)}) collective-permute-start(bf16[64,16,512]{2,1,0:T(8,128)(2,1)S(1)} %collective-permute-done.3), channel_id=1, source_target_pairs={{0,4},{4,8},{8,12},{12,16},{16,20},{20,24},{24,28},{28,0},{1,5},{5... | collective-permute-start | bytes 3145736 | tf_op jit(solution)/shard_map/ppermute | solution.py:71
  720.9 1.0 copy-start.8
  721.8 22.9 %collective-permute-start.5 = (bf16[64,16,512]{2,1,0:T(8,128)(2,1)S(1)}, bf16[64,16,512]{2,1,0:T(8,128)(2,1)}, u32[]{:S(2)}, u32[]{:S(2)}) collective-permute-start(bf16[64,16,512]{2,1,0:T(8,128)(2,1)S(1)} %collective-permute-done.4), channel_id=1, source_target_pairs={{0,4},{4,8},{8,12},{12,16},{16,20},{20,24},{24,28},{28,0},{1,5},{5... | collective-permute-start | bytes 3145736 | tf_op jit(solution)/shard_map/ppermute | solution.py:71
  744.8 21.8 %collective-permute-start.6 = (bf16[64,16,512]{2,1,0:T(8,128)(2,1)}, bf16[64,16,512]{2,1,0:T(8,128)(2,1)}, u32[]{:S(2)}, u32[]{:S(2)}) collective-permute-start(bf16[64,16,512]{2,1,0:T(8,128)(2,1)} %collective-permute-done.5), channel_id=1, source_target_pairs={{0,4},{4,8},{8,12},{12,16},{16,20},{20,24},{24,28},{28,0},{1,5},{5... | collective-permute-start | bytes 3145736 | tf_op jit(solution)/shard_map/ppermute | solution.py:71
Sparse Core Ops, SparseCore 0:
  64.1 282.3 reduce-scatter.1
  353.4 128.9 all-reduce.3
  825.0 36.3 all-reduce.5
